TPU v7x, 128 devices: a whole 4x4x4 slice. The times are simulated.
128 devices in a mesh: fsdp: 8 (over x, z_lo), dp: 16 (over z_hi, y, core).
Axes of the slice: x: 4, y: 4, z: 4 (z_hi: 2, z_lo: 2; z = z_hi * 2 + z_lo), core: 2. Of those that a mesh axis runs over, the one named last changes fastest.
Arguments:
- tokens: bfloat16 [8, 2176, 3200], P('fsdp', 'dp'), may hold values from -6 to 6
- norm_gain: float32 [3200], replicated, may hold values from 0.5 to 1.5
- qkv_weight: bfloat16 [3200, 6144], P('fsdp', 'dp'), may hold values from -4 to 4
- qk_gain: float32 [2, 2048], P(None, 'dp'), may hold values from 1 to 8
- out_weight: bfloat16 [2048, 3200], P('dp', 'fsdp'), may hold values from -0.125 to 0.125
- layer_scale: float32 [3200], replicated, may hold values from 0.2 to 1
- tile_counts: int32 [8, 2], replicated, may hold values from 0 to 2, as said below
- owners: int32 [8, 2], replicated, may hold values from 0 to 7, as said below
Outputs:
- vision_tokens: bfloat16 [32, 256, 12800], P('fsdp', None, 'dp')
Inputs may be any that keep to these rules, and one draw needn't show every extreme that they name: `tile_counts`: column 0 is 1 to 2, column 1 is 0 to 2 minus column 0. All owners together get at most 4 live tiles each, and one owner gets exactly 4.
All inputs are finite; a program needn't handle non-finite values.
Results may differ from a plain program's by a relative error of at most 0.006.
The roundings to bfloat16 on the way count: a program that leaves them out, or rounds other values in their place, can miss the bound.
Values may be sent and summed in bfloat16 or wider, within the bound.
No kernel may reach another device: no remote copies, remote signals or barrier semaphores. Data moves between devices by JAX's collectives and lax.ppermute only.
A program may use at most 192 MiB of HBM per device.

v0:
```python
import jax
import jax.numpy as jnp
from jax import lax
from jax.sharding import Mesh, PartitionSpec as P

HEAD_DIM = 128
GRID = 32
SLOTS = 2
TILE = 1025
CAP = 4
EPSILON = 1e-06


def merge_tiles(values):
    halves = GRID // 2
    columns = values.shape[1]
    tile_list = []
    for tile_slot in range(SLOTS):
        patches = values[tile_slot * TILE + 1 : (tile_slot + 1) * TILE]
        square = patches.reshape(halves, 2, halves, 2, columns).transpose(0, 2, 4, 1, 3)
        tile_list.append(square.reshape(halves * halves, columns * 4))
    return jnp.stack(tile_list)


def tile_owners(tile_counts, owners):
    slot_index = jnp.arange(SLOTS, dtype=jnp.int32)[None, :]
    first_count = tile_counts[:, 0:1]
    holder = jnp.where(slot_index < first_count, owners[:, 0:1], owners[:, 1:2])
    living = slot_index < first_count + tile_counts[:, 1:2]
    return (holder, living)


def place_tiles(received, holder, living, target):
    owned_flag = jnp.logical_and(living, holder == target).reshape(-1).astype(jnp.int32)
    before = jnp.cumsum(owned_flag) - owned_flag
    flattened = received.reshape((received.shape[0] * received.shape[1],) + received.shape[2:])
    sources = jnp.arange(flattened.shape[0], dtype=jnp.int32)
    placed = []
    for slot in range(CAP):
        match = jnp.logical_and(before == slot, owned_flag == 1)
        source = jnp.max(jnp.where(match, sources, 0))
        tile = lax.dynamic_index_in_dim(flattened, source, axis=0, keepdims=False)
        placed.append(jnp.where(jnp.any(match), tile, jnp.zeros((), tile.dtype)))
    return jnp.stack(placed)


def gather_sum(values, axis_name, groups):
    spread = jnp.broadcast_to(values[None], (groups,) + values.shape)
    collected = lax.all_to_all(spread, axis_name, split_axis=0, concat_axis=0, tiled=True)
    return jnp.sum(collected, axis=0)


def gather_blocks(block_value, axis_name, groups):
    spread = jnp.broadcast_to(block_value[None], (groups,) + block_value.shape)
    collected = lax.all_to_all(spread, axis_name, split_axis=0, concat_axis=0, tiled=True)
    return collected.reshape((groups * block_value.shape[0],) + block_value.shape[1:])


def pair_up(value, core, swap, axis):
    other = lax.ppermute(value, "core", swap)
    low = jnp.where(core == 0, value, other)
    high = jnp.where(core == 0, other, value)
    return jnp.concatenate([low, high], axis=axis)


def body(tokens, norm_gain, qkv_weight, qk_gain, out_weight, layer_scale, tile_counts, owners):
    own_rows = tokens[0]
    chips = lax.axis_size("chip")
    cores = lax.axis_size("core")
    groups = chips * cores
    chip = lax.axis_index("chip")
    core = lax.axis_index("core")
    row_index = lax.axis_index("fsdp")
    row_count = lax.axis_size("fsdp")
    model_width = own_rows.shape[1]
    block = model_width // groups
    swap = [(0, 1), (1, 0)]
    spread = jnp.broadcast_to(out_weight[None], (row_count,) + out_weight.shape)
    head_rows = lax.all_to_all(spread, "fsdp", split_axis=0, concat_axis=0, tiled=True)
    per_row = out_weight.shape[1] // block
    head_rows = head_rows.reshape(row_count, HEAD_DIM, per_row, block).transpose(0, 2, 1, 3)
    weight_block = lax.all_to_all(
        head_rows.reshape(groups, HEAD_DIM, block),
        ("chip", "core"),
        split_axis=0,
        concat_axis=0,
        tiled=True,
    ).reshape(groups * HEAD_DIM, block)
    pair_weight = pair_up(weight_block, core, swap, 1)
    full_qkv = gather_blocks(qkv_weight, "fsdp", row_count)
    pair_qkv = pair_up(full_qkv, core, swap, 1)
    pair_qkv, pair_weight = lax.optimization_barrier((pair_qkv, pair_weight))
    pair_gain = pair_up(qk_gain, core, swap, 1).reshape(2, cores, HEAD_DIM)
    half = lax.all_gather(own_rows, "chip", axis=0, tiled=True)
    half_length = half.shape[0]
    piece = own_rows.shape[0]
    values = half.astype(jnp.float32)
    normed = (
        values * lax.rsqrt(jnp.mean(values * values, axis=-1, keepdims=True) + EPSILON) * norm_gain
    ).astype(jnp.bfloat16)
    projected = jnp.dot(normed, pair_qkv, preferred_element_type=jnp.float32)
    projected = projected.reshape(half_length, cores, 3, HEAD_DIM)
    queries = projected[:, :, 0]
    keys_part = projected[:, :, 1]
    values_part = projected[:, :, 2].astype(jnp.bfloat16)
    sums = gather_sum(
        jnp.stack(
            [jnp.sum(queries * queries, axis=(1, 2)), jnp.sum(keys_part * keys_part, axis=(1, 2))]
        ),
        "chip",
        chips,
    )
    window = groups * HEAD_DIM
    queries = (
        queries * lax.rsqrt(sums[0] / window + EPSILON)[:, None, None] * pair_gain[0][None]
    ).astype(jnp.bfloat16)
    keys_part = (
        keys_part * lax.rsqrt(sums[1] / window + EPSILON)[:, None, None] * pair_gain[1][None]
    ).astype(jnp.bfloat16)
    stacked = jnp.stack([queries, keys_part, values_part])
    mine = lax.dynamic_index_in_dim(stacked, core, axis=2, keepdims=False)
    theirs = lax.dynamic_index_in_dim(stacked, 1 - core, axis=2, keepdims=False)
    got = lax.ppermute(theirs, "core", swap)
    first_half = jnp.where(core == 0, mine, got).reshape(3, chips, piece, HEAD_DIM)
    second_half = jnp.where(core == 0, got, mine).reshape(3, chips, piece, HEAD_DIM)
    whole = jnp.stack([first_half, second_half], axis=2).reshape(3, groups * piece, HEAD_DIM)
    length = whole.shape[1]
    factor = HEAD_DIM ** (-0.5)
    covered = SLOTS * TILE
    tile_query = whole[0, :covered].reshape(SLOTS, TILE, HEAD_DIM)
    tile_key = whole[1, :covered].reshape(SLOTS, TILE, HEAD_DIM)
    tile_value = whole[2, :covered].reshape(SLOTS, TILE, HEAD_DIM)
    scores = (
        jnp.einsum("sqc,skc->sqk", tile_query, tile_key, preferred_element_type=jnp.float32)
        * factor
    )
    highest = jnp.max(scores, axis=-1, keepdims=True)
    exponent = jnp.exp(scores - highest)
    weights = (exponent / jnp.sum(exponent, axis=-1, keepdims=True)).astype(jnp.bfloat16)
    tile_out = jnp.einsum(
        "sqk,skc->sqc", weights, tile_value, preferred_element_type=jnp.float32
    ).astype(jnp.bfloat16)
    head_out = jnp.concatenate(
        [
            tile_out.reshape(covered, HEAD_DIM),
            jnp.zeros((length - covered, HEAD_DIM), jnp.bfloat16),
        ],
        axis=0,
    )
    by_half = head_out.reshape(chips, cores, piece, HEAD_DIM).transpose(1, 0, 2, 3)
    by_half = by_half.reshape(cores, half_length, HEAD_DIM)
    outgoing = jnp.broadcast_to(by_half[None], (chips, cores, half_length, HEAD_DIM))
    all_heads = lax.all_to_all(
        outgoing.reshape(groups, half_length, HEAD_DIM),
        ("chip", "core"),
        split_axis=0,
        concat_axis=0,
        tiled=True,
    )
    head_terms = jnp.einsum(
        "hsc,hcd->hsd",
        all_heads,
        pair_weight.reshape(groups, HEAD_DIM, cores * block),
        preferred_element_type=jnp.float32,
    ).astype(jnp.bfloat16)
    attention = jnp.sum(lax.optimization_barrier(head_terms).astype(jnp.float32), axis=0)
    pair_tokens = lax.dynamic_slice_in_dim(half, chip * cores * block, cores * block, axis=1)
    pair_scale = lax.dynamic_slice_in_dim(layer_scale, chip * cores * block, cores * block)
    updated_half = (pair_tokens.astype(jnp.float32) + pair_scale * attention).astype(jnp.bfloat16)
    keep = lax.dynamic_slice_in_dim(updated_half, core * block, block, axis=1)
    give = lax.dynamic_slice_in_dim(updated_half, (1 - core) * block, block, axis=1)
    taken = lax.ppermute(give, "core", swap)
    first_half = jnp.where(core == 0, keep, taken).reshape(chips, piece, block)
    second_half = jnp.where(core == 0, taken, keep).reshape(chips, piece, block)
    updated = jnp.stack([first_half, second_half], axis=1).reshape(length, block)
    merged = merge_tiles(updated)
    holder, living = tile_owners(tile_counts, owners)
    own_holder = holder[row_index]
    own_living = living[row_index]
    destination = jnp.arange(row_count, dtype=jnp.int32)[:, None]
    sending = jnp.logical_and(destination == own_holder[None, :], own_living[None, :])
    outgoing = jnp.where(sending[:, :, None, None], merged[None], jnp.zeros((), jnp.bfloat16))
    received = lax.all_to_all(outgoing, "fsdp", split_axis=0, concat_axis=0, tiled=True)
    return place_tiles(received, holder, living, row_index)


def solution(mesh):
    fsdp_size = mesh.shape["fsdp"]
    dp_size = mesh.shape["dp"]
    split = Mesh(mesh.devices.reshape(fsdp_size, dp_size // 2, 2), ("fsdp", "chip", "core"))
    heads = ("chip", "core")
    placed = (
        P("fsdp", heads, None),
        P(),
        P("fsdp", heads),
        P(None, heads),
        P(heads, "fsdp"),
        P(),
        P(),
        P(),
    )
    return jax.shard_map(
        body, mesh=split, in_specs=placed, out_specs=P("fsdp", None, heads), check_vma=False
    )
```

profile of v0, /device:TPU:8, one launch (start us, length us, event | category | flops | bytes accessed | tf_op | source)
XLA Modules:
  0.0 395.8 jit_solution(15600557721737662386)
XLA Ops:
  8.3 19.0 %all_to_all.30 = bf16[8,128,400]{1,2,0:T(8,128)(2,1)S(1)} all-to-all(bf16[8,128,400]{1,2,0:T(8,128)(2,1)S(1)} %broadcast_in_dim.95), channel_id=1, replica_groups=mesh['fsdp'=8,'chip'=8,'core'=2] {'fsdp'}, dimensions={0} | all-to-all | bytes 1638400 | tf_op jit(solution)/shard_map/all_to_all | solution.py:79
  29.0 3.6 all-to-all-start
  36.4 30.7 %all-to-all-done = bf16[8,400,384]{2,1,0:T(8,128)(2,1)S(1)} async-done(((bf16[8,400,384]{2,1,0:T(8,128)(2,1)}), bf16[8,400,384]{2,1,0:T(8,128)(2,1)S(1)}, u32[]{:S(2)}, u32[]{:S(2)}) %all-to-all-start) | async-done | bytes 2457632 | tf_op jit(solution)/shard_map/all_to_all | solution.py:55
  67.1 8.0 %all-to-all-start.2 = ((bf16[16,128,200]{1,2,0:T(8,128)(2,1)}), bf16[16,128,200]{1,2,0:T(8,128)(2,1)S(1)}, u32[]{:S(2)}, u32[]{:S(2)}) async-start(bf16[16,128,200]{1,2,0:T(8,128)(2,1)} %copy.108), calls=%async_computation.2 | async-start | bytes 1638400 | tf_op jit(solution)/shard_map/all_to_all | solution.py:82
  75.2 15.0 %all-to-all-done.2 = bf16[16,128,200]{1,2,0:T(8,128)(2,1)S(1)} async-done(((bf16[16,128,200]{1,2,0:T(8,128)(2,1)}), bf16[16,128,200]{1,2,0:T(8,128)(2,1)S(1)}, u32[]{:S(2)}, u32[]{:S(2)}) %all-to-all-start.2) | async-done | bytes 819232 | tf_op jit(solution)/shard_map/all_to_all | solution.py:82
  102.2 26.1 %all-gather.3.cloned.1.call-done = bf16[1,1088,3200]{2,1,0:T(8,128)(2,1)} async-done(((bf16[1,136,3200]{2,1,0:T(8,128)(2,1)}), bf16[1,1088,3200]{2,1,0:T(8,128)(2,1)}) %all-gather.3.cloned.1.call-update) | async-done | bytes 6963216 | tf_op jit(solution)/shard_map/all_gather | solution.py:94
  128.3 4.6 %fusion.2 = f32[1088]{0:T(1024)S(1)} fusion(bf16[1,1088,3200]{2,1,0:T(8,128)(2,1)} %all-gather.3.cloned.1.call-done), kind=kLoop, calls=%fused_computation.7 | loop fusion | flops 10443712 | bytes 6967552 | tf_op jit(solution)/shard_map/reduce_sum | solution.py:99
  133.3 9.5 %fusion.6 = f32[1088,768]{0,1:T(8,128)S(1)} fusion(bf16[3200,768]{1,0:T(8,128)(2,1)} %pad_maximum_fusion, bf16[1,1088,3200]{2,1,0:T(8,128)(2,1)S(1)} %copy-done, f32[3200]{0:T(1024)S(1)} %copy-done.8, f32[1088]{0:T(1024)S(1)} %add_rsqrt_fusion), kind=kOutput, calls=%fused_computation.12 | convolution fusion | flops 5361664000 | bytes 15237888 | tf_op jit(solution)/shard_map/dot_general | solution.py:101
  143.8 5.6 %all-to-all-start.3 = ((f32[8,2,1088]{2,1,0:T(2,128)}), f32[8,2,1088]{2,1,0:T(2,128)}, u32[]{:S(2)}, u32[]{:S(2)}) async-start(f32[8,2,1088]{2,1,0:T(2,128)} %broadcast_in_dim.96), calls=%async_computation.3 | async-start | bytes 147456 | tf_op jit(solution)/shard_map/all_to_all | solution.py:49
  150.3 5.9 %all-to-all-done.3 = f32[8,2,1088]{2,1,0:T(2,128)} async-done(((f32[8,2,1088]{2,1,0:T(2,128)}), f32[8,2,1088]{2,1,0:T(2,128)}, u32[]{:S(2)}, u32[]{:S(2)}) %all-to-all-start.3) | async-done | bytes 69664 | tf_op jit(solution)/shard_map/all_to_all | solution.py:49
  162.9 3.2 fusion.45
  166.2 4.9 %fusion.12 = bf16[2,1025,128]{2,1,0:T(8,128)(2,1)S(1)} fusion(bf16[2,1025,128]{2,1,0:T(8,128)(2,1)S(1)} %reshape_squeeze.11, f32[2,1025]{1,0:T(2,128)S(1)} %fusion.45, bf16[2,1025,128]{2,1,0:T(8,128)(2,1)S(1)} %reshape_squeeze.9, bf16[2,1025,128]{2,1,0:T(8,128)(2,1)S(1)} %reshape_squeeze.10), kind=kOutput, calls=%fused_computation.19 | convolution fusion | flops 1084510464 | bytes 2107400 | tf_op jit(solution)/shard_map/sqk,skc->sqc/dot_general | solution.py:140
  174.3 5.7 %all-to-all-start.4 = ((bf16[16,1088,128]{2,1,0:T(8,128)(2,1)}), bf16[16,1088,128]{2,1,0:T(8,128)(2,1)}, u32[]{:S(2)}, u32[]{:S(2)}) async-start(bf16[16,1088,128]{2,1,0:T(8,128)(2,1)} %bitcast.100), calls=%async_computation.4 | async-start | bytes 8912896 | tf_op jit(solution)/shard_map/all_to_all | solution.py:153
  184.5 55.5 %all-to-all-done.4 = bf16[16,1088,128]{2,1,0:T(8,128)(2,1)} async-done(((bf16[16,1088,128]{2,1,0:T(8,128)(2,1)}), bf16[16,1088,128]{2,1,0:T(8,128)(2,1)}, u32[]{:S(2)}, u32[]{:S(2)}) %all-to-all-start.4) | async-done | bytes 4456480 | tf_op jit(solution)/shard_map/all_to_all | solution.py:153
  240.0 11.4 %convolution_convert_fusion = bf16[16,1088,400]{1,2,0:T(8,128)(2,1)} fusion(bf16[16,1088,128]{2,1,0:T(8,128)(2,1)} %all-to-all-done.4, bf16[2048,400]{0,1:T(8,128)(2,1)S(1)} %copy-done.1), kind=kOutput, calls=%fused_computation.2 | convolution fusion | flops 1789542400 | bytes 20021248 | tf_op jit(solution)/shard_map/hsc,hcd->hsd/dot_general | solution.py:160
  251.4 7.8 %convert_reduce_fusion = f32[1088,400]{0,1:T(8,128)S(1)} fusion(bf16[16,1088,400]{1,2,0:T(8,128)(2,1)} %convolution_convert_fusion), kind=kLoop, calls=%fused_computation.1 | loop fusion | flops 13491200 | bytes 15667200 | tf_op jit(solution)/shard_map/reduce_sum | solution.py:166
  265.1 4.9 %copy.125 = bf16[16,16,200,2,2]{1,0,4,3,2:T(8,128)(2,1)S(1)} copy(bf16[16,16,200,2,2]{2,4,1,3,0:T(2,128)(2,1)} %bitcast.115) | data formatting | bytes 819200 | tf_op jit(solution)/shard_map/transpose | solution.py:20
  270.0 3.9 stack_reshape.23
  273.8 4.9 %copy.124 = bf16[16,16,200,2,2]{1,0,4,3,2:T(8,128)(2,1)S(1)} copy(bf16[16,16,200,2,2]{2,4,1,3,0:T(2,128)(2,1)} %bitcast.114) | data formatting | bytes 819200 | tf_op jit(solution)/shard_map/transpose | solution.py:20
  278.7 3.8 stack_reshape.22
  283.8 3.3 broadcast_select_fusion
  287.1 4.8 %all-to-all-start.5 = ((bf16[8,2,256,800]{2,3,1,0:T(8,128)(2,1)}), bf16[8,2,256,800]{2,3,1,0:T(8,128)(2,1)}, u32[]{:S(2)}, u32[]{:S(2)}) async-start(bf16[8,2,256,800]{2,3,1,0:T(8,128)(2,1)} %broadcast_select_fusion), calls=%async_computation.5 | async-start | bytes 13107200 | tf_op jit(solution)/shard_map/all_to_all | solution.py:183
  302.7 80.9 %all-to-all-done.5 = bf16[8,2,256,800]{2,3,1,0:T(8,128)(2,1)} async-done(((bf16[8,2,256,800]{2,3,1,0:T(8,128)(2,1)}), bf16[8,2,256,800]{2,3,1,0:T(8,128)(2,1)}, u32[]{:S(2)}, u32[]{:S(2)}) %all-to-all-start.5) | async-done | bytes 6553632 | tf_op jit(solution)/shard_map/all_to_all | solution.py:183
  383.6 4.0 %dynamic-slice_select_fusion.3 = (bf16[1,256,800]{1,2,0:T(8,128)(2,1)S(1)}, bf16[1,256,800]{1,2,0:T(8,128)(2,1)S(1)}, bf16[1,256,800]{1,2,0:T(8,128)(2,1)S(1)}, bf16[1,256,800]{1,2,0:T(8,128)(2,1)S(1)}) fusion(bf16[16,256,800]{1,2,0:T(8,128)(2,1)} %bitcast.30, s32[]{:T(128)S(6)} %select_n.180, pred[]{:T(512)} %get-tuple-element.44, s32[]{:T(128)S(6)} %select_n.192, ...), kind=kLoop, calls=%fused_computation.54 | loop fusion | flops 819200 | bytes 3276820 | tf_op jit(solution)/shard_map/jit(_where)/select_n | solution.py:43
  (100 shorter events, 47.3 us)
Async XLA Ops:
  6.5 20.7 %copy-start.4 = (bf16[400,384]{1,0:T(8,128)(2,1)S(1)}, bf16[400,384]{1,0:T(8,128)(2,1)}, u32[]{:S(2)}) copy-start(bf16[400,384]{1,0:T(8,128)(2,1)} %param.10) | copy-start | bytes 921604
  6.5 121.8 %all-gather.3.cloned.1.call-start = ((), (), s32[]{:S(2)}) async-start(), calls=%async_computation.6 | async-start | bytes 7833600 | tf_op jit(solution)/shard_map/all_gather | solution.py:94
  29.0 38.1 %all-to-all-start = ((bf16[8,400,384]{2,1,0:T(8,128)(2,1)}), bf16[8,400,384]{2,1,0:T(8,128)(2,1)S(1)}, u32[]{:S(2)}, u32[]{:S(2)}) async-start(bf16[8,400,384]{2,1,0:T(8,128)(2,1)} %broadcast_in_dim.94), calls=%async_computation | async-start | bytes 4915200 | tf_op jit(solution)/shard_map/all_to_all | solution.py:55
  34.1 57.7 %copy-start.7 = (f32[2,128]{1,0:T(2,128)S(1)}, f32[2,128]{1,0:T(2,128)}, u32[]{:S(2)}) copy-start(f32[2,128]{1,0:T(2,128)} %param.11) | copy-start | bytes 3076
  67.1 23.1 %all-to-all-start.2 = ((bf16[16,128,200]{1,2,0:T(8,128)(2,1)}), bf16[16,128,200]{1,2,0:T(8,128)(2,1)S(1)}, u32[]{:S(2)}, u32[]{:S(2)}) async-start(bf16[16,128,200]{1,2,0:T(8,128)(2,1)} %copy.108), calls=%async_computation.2 | async-start | bytes 1638400 | tf_op jit(solution)/shard_map/all_to_all | solution.py:82
  75.1 22.3 %collective-permute-start = (bf16[3200,384]{1,0:T(8,128)(2,1)S(1)}, bf16[3200,384]{1,0:T(8,128)(2,1)}, u32[]{:S(2)}, u32[]{:S(2)}) collective-permute-start(bf16[3200,384]{1,0:T(8,128)(2,1)S(1)} %bitcast.101), channel_id=1, source_target_pairs={{0,1},{1,0},{2,3},{3,2},{4,5},{5,4},{6,7},{7,6},{8,9},{9,8},{10,11... | collective-permute-start | bytes 7372808 | tf_op jit(solution)/shard_map/ppermute | solution.py:60
  91.1 3.5 collective-permute-start.1
  91.8 2.3 collective-permute-start.2
  128.3 5.0 %copy-start = (bf16[1,1088,3200]{2,1,0:T(8,128)(2,1)S(1)}, bf16[1,1088,3200]{2,1,0:T(8,128)(2,1)}, u32[]{:S(2)}) copy-start(bf16[1,1088,3200]{2,1,0:T(8,128)(2,1)} %all-gather.3.cloned.1.call-done) | copy-start | bytes 20889604
  128.3 5.0 %copy-start.8 = (f32[3200]{0:T(1024)S(1)}, f32[3200]{0:T(1024)}, u32[]{:S(2)}) copy-start(f32[3200]{0:T(1024)} %param.9) | copy-start | bytes 38404
  143.8 12.4 %all-to-all-start.3 = ((f32[8,2,1088]{2,1,0:T(2,128)}), f32[8,2,1088]{2,1,0:T(2,128)}, u32[]{:S(2)}, u32[]{:S(2)}) async-start(f32[8,2,1088]{2,1,0:T(2,128)} %broadcast_in_dim.96), calls=%async_computation.3 | async-start | bytes 147456 | tf_op jit(solution)/shard_map/all_to_all | solution.py:49
  157.1 1.1 copy-start.3
  159.4 2.6 collective-permute-start.3
  174.3 6.6 %copy-start.5 = (s32[8,2]{0,1:T(2,128)S(1)}, s32[8,2]{0,1:T(2,128)}, u32[]{:S(2)}) copy-start(s32[8,2]{0,1:T(2,128)} %param.14) | copy-start | bytes 196
  174.3 6.6 %copy-start.6 = (s32[8,2]{0,1:T(2,128)S(1)}, s32[8,2]{0,1:T(2,128)}, u32[]{:S(2)}) copy-start(s32[8,2]{0,1:T(2,128)} %param.15) | copy-start | bytes 196
  174.3 65.7 %all-to-all-start.4 = ((bf16[16,1088,128]{2,1,0:T(8,128)(2,1)}), bf16[16,1088,128]{2,1,0:T(8,128)(2,1)}, u32[]{:S(2)}, u32[]{:S(2)}) async-start(bf16[16,1088,128]{2,1,0:T(8,128)(2,1)} %bitcast.100), calls=%async_computation.4 | async-start | bytes 8912896 | tf_op jit(solution)/shard_map/all_to_all | solution.py:153
  180.0 60.0 %copy-start.1 = (bf16[2048,400]{0,1:T(8,128)(2,1)S(1)}, bf16[2048,400]{0,1:T(8,128)(2,1)}, u32[]{:S(2)}) copy-start(bf16[2048,400]{0,1:T(8,128)(2,1)} %pad_maximum_fusion.3) | copy-start | bytes 4915204
  251.4 7.8 %copy-start.2 = (bf16[1,1088,400]{1,2,0:T(8,128)(2,1)S(1)}, bf16[1,1088,400]{1,2,0:T(8,128)(2,1)}, u32[]{:S(2)}) copy-start(bf16[1,1088,400]{1,2,0:T(8,128)(2,1)} %copy.130) | copy-start | bytes 2611204
  259.6 2.2 collective-permute-start.4
  287.1 96.5 %all-to-all-start.5 = ((bf16[8,2,256,800]{2,3,1,0:T(8,128)(2,1)}), bf16[8,2,256,800]{2,3,1,0:T(8,128)(2,1)}, u32[]{:S(2)}, u32[]{:S(2)}) async-start(bf16[8,2,256,800]{2,3,1,0:T(8,128)(2,1)} %broadcast_select_fusion), calls=%async_computation.5 | async-start | bytes 13107200 | tf_op jit(solution)/shard_map/all_to_all | solution.py:183
Sparse Core Ops, SparseCore 0:
  9.7 118.6 all-gather.2
where the time goes:
time: 397 us; the launch traced here: 396 us
  waiting for transfers between devices  220 us (55%)
  local copies, waits for them, and re-layouts  39.9 us (10%)
  other arithmetic  36.9 us (9%)
  starting transfers between devices  29.1 us (7%)
  matrix products  29 us (7%)
  between operations  21.5 us (5%)
  blocking collectives  19 us (5%)
    all_to_all x1, waiting for transfers between devices, body(): lax.all_to_all(outgoing, 'fsdp', split_axis=0, concat_axis=0, tiled=True)  80.9 us
    all_to_all x1, waiting for transfers between devices, body(): lax.all_to_all(outgoing.reshape(groups, half_length, HEAD_DIM), ('chip',...  55.5 us
    all_to_all x1, waiting for transfers between devices, gather_blocks(): lax.all_to_all(spread, axis_name, split_axis=0, concat_axis=0, tiled=True)  30.7 us
    all_gather x1, waiting for transfers between devices, body(): half = lax.all_gather(own_rows, 'chip', axis=0, tiled=True)  26.1 us
    all_to_all x1, blocking collectives, body(): lax.all_to_all(spread, 'fsdp', split_axis=0, concat_axis=0, tiled=True)  19 us
    all_to_all x1, waiting for transfers between devices, body(): lax.all_to_all(head_rows.reshape(groups, HEAD_DIM, block), ('chip', 'core...  15 us
    dot_general x1, matrix products, body(): jnp.einsum('hsc,hcd->hsd', all_heads, pair_weight.reshape(groups, HEAD_DI...  11.4 us
    transpose x2, local copies, waits for them, and re-layouts, merge_tiles(): patches.reshape(halves, 2, halves, 2, columns).transpose(0, 2, 4, 1, 3)  9.74 us
  transfers between devices with their start and end apart: 11, of which 9 were waited for; matrix products, arithmetic and copies ran while one was open for 6% of the time, Pallas kernels for 0%

commit v1 on v0

--- a/solution.py
+++ b/solution.py
@@ -2,6 +2,7 @@
 import jax.numpy as jnp
 from jax import lax
 from jax.sharding import Mesh, PartitionSpec as P
+from jax.lax import all_to_all, axis_size
 
 HEAD_DIM = 128
 GRID = 32
@@ -91,7 +92,9 @@
     pair_qkv = pair_up(full_qkv, core, swap, 1)
     pair_qkv, pair_weight = lax.optimization_barrier((pair_qkv, pair_weight))
     pair_gain = pair_up(qk_gain, core, swap, 1).reshape(2, cores, HEAD_DIM)
-    half = lax.all_gather(own_rows, "chip", axis=0, tiled=True)
+    s_next = jnp.stack([own_rows for _ in range(axis_size("chip"))])
+    odd = all_to_all(s_next, "chip", 0, 0)
+    half = jnp.concatenate(odd, axis=0)
     half_length = half.shape[0]
     piece = own_rows.shape[0]
     values = half.astype(jnp.float32)

time: 397 us -> 455 us (1.15)
  blocking collectives: 19 us -> 74 us
  between operations: 21.5 us -> 8.41 us
  waiting for transfers between devices: 220 us -> 228 us
  local copies, waits for them, and re-layouts: 39.9 us -> 44.5 us
    all_to_all x0 -> x2, blocking collectives: none -> 55.1 us  [the longest x1 34.6 us: gather_blocks(): lax.all_to_all(spread, axis_name, split_axis=0, concat_axis=0, tiled=True)]
    all_to_all x2 -> x1, waiting for transfers between devices: 45.7 us -> 77.2 us  [body(): odd = all_to_all(s_next, 'chip', 0, 0)]
    all_gather x1 -> x0, waiting for transfers between devices: 26.1 us -> none  [body(): half = lax.all_gather(own_rows, 'chip', axis=0, tiled=True)]
    dot_general x0 -> x1, local copies, waits for them, and re-layouts: none -> 7.43 us  [body(): projected = jnp.dot(normed, pair_qkv, preferred_element_type=jnp.float32)]
    convert_element_type x0 -> x1, other arithmetic: none -> 5.67 us  [body(): normed = (values * lax.rsqrt(jnp.mean(values * values, axis=-1, keepdims=...]
    all_to_all x2 -> x1, starting transfers between devices: 11.6 us -> 6.64 us  [body(): odd = all_to_all(s_next, 'chip', 0, 0)]
  transfers between devices with their start and end apart: 11 -> 9, of which waited for: 9 -> 7; matrix products, arithmetic and copies ran while one was open for 6% -> 5% of each run, Pallas kernels for 0% -> 0%
where the time goes in v1:
time: 455 us; the launch traced here: 450 us
  waiting for transfers between devices  228 us (50%)
  blocking collectives  74 us (16%)
  local copies, waits for them, and re-layouts  44.5 us (10%)
  other arithmetic  40.5 us (9%)
  starting transfers between devices  27.8 us (6%)
  matrix products  27.7 us (6%)
  between operations  8.41 us (2%)
    all_to_all x1, waiting for transfers between devices, body(): lax.all_to_all(outgoing, 'fsdp', split_axis=0, concat_axis=0, tiled=True)  80.9 us
    all_to_all x1, waiting for transfers between devices, body(): odd = all_to_all(s_next, 'chip', 0, 0)  77.2 us
    all_to_all x1, waiting for transfers between devices, body(): lax.all_to_all(outgoing.reshape(groups, half_length, HEAD_DIM), ('chip',...  55.5 us
    all_to_all x1, blocking collectives, gather_blocks(): lax.all_to_all(spread, axis_name, split_axis=0, concat_axis=0, tiled=True)  34.6 us
    all_to_all x1, blocking collectives, body(): lax.all_to_all(head_rows.reshape(groups, HEAD_DIM, block), ('chip', 'core...  20.4 us
    all_to_all x1, blocking collectives, body(): lax.all_to_all(spread, 'fsdp', split_axis=0, concat_axis=0, tiled=True)  18.9 us
    dot_general x1, matrix products, body(): jnp.einsum('hsc,hcd->hsd', all_heads, pair_weight.reshape(groups, HEAD_DI...  11.4 us
    transpose x2, local copies, waits for them, and re-layouts, merge_tiles(): patches.reshape(halves, 2, halves, 2, columns).transpose(0, 2, 4, 1, 3)  9.74 us
  transfers between devices with their start and end apart: 9, of which 7 were waited for; matrix products, arithmetic and copies ran while one was open for 5% of the time, Pallas kernels for 0%

profile of v1, /device:TPU:8, one launch (start us, length us, event | category | flops | bytes accessed | tf_op | source)
XLA Modules:
  0.0 450.5 jit_solution(17022489450399082636)
XLA Ops:
  1.0 18.9 %all_to_all.35 = bf16[8,128,400]{1,2,0:T(8,128)(2,1)S(1)} all-to-all(bf16[8,128,400]{1,2,0:T(8,128)(2,1)S(1)} %broadcast_in_dim.95), channel_id=1, replica_groups=mesh['fsdp'=8,'chip'=8,'core'=2] {'fsdp'}, dimensions={0} | all-to-all | bytes 1638400 | tf_op jit(solution)/shard_map/all_to_all | solution.py:80
  20.7 20.4 %all_to_all.36 = bf16[16,128,200]{1,2,0:T(8,128)(2,1)S(1)} all-to-all(bf16[16,128,200]{1,2,0:T(8,128)(2,1)S(1)} %copy.81), channel_id=1, replica_groups=mesh['fsdp'=8,'chip'=8,'core'=2] {'chip','core'}, dimensions={0} | all-to-all | bytes 1638400 | tf_op jit(solution)/shard_map/all_to_all | solution.py:83
  41.4 34.6 %all_to_all.37 = bf16[8,400,384]{2,1,0:T(8,128)(2,1)S(1)} all-to-all(bf16[8,400,384]{2,1,0:T(8,128)(2,1)S(1)} %broadcast_in_dim.94), channel_id=1, replica_groups=mesh['fsdp'=8,'chip'=8,'core'=2] {'fsdp'}, dimensions={0} | all-to-all | bytes 4915200 | tf_op jit(solution)/shard_map/all_to_all | solution.py:56
  79.4 6.6 %all-to-all-start = ((bf16[8,136,3200]{2,1,0:T(8,128)(2,1)}), bf16[8,136,3200]{2,1,0:T(8,128)(2,1)}, u32[]{:S(2)}, u32[]{:S(2)}) async-start(bf16[8,136,3200]{2,1,0:T(8,128)(2,1)} %stack.34), calls=%async_computation | async-start | bytes 13926400 | tf_op jit(solution)/shard_map/all_to_all | solution.py:96
  87.9 4.2 collective-permute-done.2
  99.6 7.4 %copy.83 = bf16[768,3200]{1,0:T(8,128)(2,1)} copy(bf16[768,3200]{0,1:T(8,128)(2,1)} %bitcast.105) | data formatting | bytes 9830400 | tf_op jit(solution)/shard_map/dot_general | solution.py:104
  107.0 77.2 %all-to-all-done = bf16[8,136,3200]{2,1,0:T(8,128)(2,1)} async-done(((bf16[8,136,3200]{2,1,0:T(8,128)(2,1)}), bf16[8,136,3200]{2,1,0:T(8,128)(2,1)}, u32[]{:S(2)}, u32[]{:S(2)}) %all-to-all-start) | async-done | bytes 6963232 | tf_op jit(solution)/shard_map/all_to_all | solution.py:96
  184.2 4.4 fusion.2
  188.7 5.7 %fusion.4 = bf16[8,136,3200]{2,1,0:T(8,128)(2,1)S(1)} fusion(bf16[8,136,3200]{2,1,0:T(8,128)(2,1)} %all-to-all-done, f32[3200]{0:T(1024)S(1)} %copy-done.5, f32[8,136]{1,0:T(8,128)S(1)} %add_rsqrt_fusion), kind=kLoop, calls=%fused_computation.9 | loop fusion | flops 13926400 | bytes 13943552 | tf_op jit(solution)/shard_map/convert_element_type | solution.py:103
  194.3 8.2 %fusion.41 = f32[1088,2,3,128]{3,0,2,1:T(8,128)S(1)} fusion(bf16[1088,3200,1,1]{1,0,3,2:T(8,128)(2,1)S(1)} %bitcast.108, bf16[2,3,128,3200]{3,2,1,0:T(8,128)(2,1)} %bitcast.110), kind=kOutput, calls=%fused_computation.105 | convolution fusion | flops 5347737600 | bytes 15220736 | tf_op jit(solution)/shard_map/dot_general | solution.py:104
  203.7 8.7 %all-to-all-start.4 = ((f32[8,2,1088]{2,1,0:T(2,128)}), f32[8,2,1088]{2,1,0:T(2,128)S(1)}, u32[]{:S(2)}, u32[]{:S(2)}) async-start(f32[8,2,1088]{2,1,0:T(2,128)} %broadcast_in_dim.96), calls=%async_computation.4 | async-start | bytes 147456 | tf_op jit(solution)/shard_map/all_to_all | solution.py:50
  213.2 5.7 %all-to-all-done.4 = f32[8,2,1088]{2,1,0:T(2,128)S(1)} async-done(((f32[8,2,1088]{2,1,0:T(2,128)}), f32[8,2,1088]{2,1,0:T(2,128)S(1)}, u32[]{:S(2)}, u32[]{:S(2)}) %all-to-all-start.4) | async-done | bytes 69664 | tf_op jit(solution)/shard_map/all_to_all | solution.py:50
  227.2 4.9 %fusion.7 = bf16[2,1025,128]{2,1,0:T(8,128)(2,1)S(1)} fusion(bf16[2,1025,128]{2,1,0:T(8,128)(2,1)S(1)} %reshape_squeeze.11, f32[2,1025]{1,0:T(2,128)S(1)} %fusion.40, bf16[2,1025,128]{2,1,0:T(8,128)(2,1)S(1)} %reshape_squeeze.9, bf16[2,1025,128]{2,1,0:T(8,128)(2,1)S(1)} %reshape_squeeze.10), kind=kOutput, calls=%fused_computation.15 | convolution fusion | flops 1084510464 | bytes 2107400 | tf_op jit(solution)/shard_map/sqk,skc->sqc/dot_general | solution.py:143
  235.3 6.0 %all-to-all-start.5 = ((bf16[16,1088,128]{2,1,0:T(8,128)(2,1)}), bf16[16,1088,128]{2,1,0:T(8,128)(2,1)}, u32[]{:S(2)}, u32[]{:S(2)}) async-start(bf16[16,1088,128]{2,1,0:T(8,128)(2,1)} %bitcast.106), calls=%async_computation.5 | async-start | bytes 8912896 | tf_op jit(solution)/shard_map/all_to_all | solution.py:156
  245.9 55.5 %all-to-all-done.5 = bf16[16,1088,128]{2,1,0:T(8,128)(2,1)} async-done(((bf16[16,1088,128]{2,1,0:T(8,128)(2,1)}), bf16[16,1088,128]{2,1,0:T(8,128)(2,1)}, u32[]{:S(2)}, u32[]{:S(2)}) %all-to-all-start.5) | async-done | bytes 4456480 | tf_op jit(solution)/shard_map/all_to_all | solution.py:156
  301.4 11.4 %convolution_convert_fusion = bf16[16,1088,400]{1,2,0:T(8,128)(2,1)} fusion(bf16[16,1088,128]{2,1,0:T(8,128)(2,1)} %all-to-all-done.5, bf16[2048,400]{0,1:T(8,128)(2,1)S(1)} %copy-done), kind=kOutput, calls=%fused_computation.2 | convolution fusion | flops 1789542400 | bytes 20021248 | tf_op jit(solution)/shard_map/hsc,hcd->hsd/dot_general | solution.py:163
  312.8 7.8 %convert_reduce_fusion = f32[1088,400]{0,1:T(8,128)S(1)} fusion(bf16[16,1088,400]{1,2,0:T(8,128)(2,1)} %convolution_convert_fusion), kind=kLoop, calls=%fused_computation.1 | loop fusion | flops 13491200 | bytes 15667200 | tf_op jit(solution)/shard_map/reduce_sum | solution.py:169
  326.4 4.9 %copy.94 = bf16[16,16,200,2,2]{1,0,4,3,2:T(8,128)(2,1)S(1)} copy(bf16[16,16,200,2,2]{2,4,1,3,0:T(2,128)(2,1)} %bitcast.119) | data formatting | bytes 819200 | tf_op jit(solution)/shard_map/transpose | solution.py:21
  331.3 3.9 stack_reshape.23
  335.1 4.9 %copy.93 = bf16[16,16,200,2,2]{1,0,4,3,2:T(8,128)(2,1)S(1)} copy(bf16[16,16,200,2,2]{2,4,1,3,0:T(2,128)(2,1)} %bitcast.118) | data formatting | bytes 819200 | tf_op jit(solution)/shard_map/transpose | solution.py:21
  340.0 3.8 stack_reshape.22
  348.4 4.8 %all-to-all-start.6 = ((bf16[8,2,256,800]{2,3,1,0:T(8,128)(2,1)}), bf16[8,2,256,800]{2,3,1,0:T(8,128)(2,1)}, u32[]{:S(2)}, u32[]{:S(2)}) async-start(bf16[8,2,256,800]{2,3,1,0:T(8,128)(2,1)} %broadcast_select_fusion), calls=%async_computation.6 | async-start | bytes 13107200 | tf_op jit(solution)/shard_map/all_to_all | solution.py:186
  364.0 80.9 %all-to-all-done.6 = bf16[8,2,256,800]{2,3,1,0:T(8,128)(2,1)} async-done(((bf16[8,2,256,800]{2,3,1,0:T(8,128)(2,1)}), bf16[8,2,256,800]{2,3,1,0:T(8,128)(2,1)}, u32[]{:S(2)}, u32[]{:S(2)}) %all-to-all-start.6) | async-done | bytes 6553632 | tf_op jit(solution)/shard_map/all_to_all | solution.py:186
  444.9 4.0 dynamic-slice_select_fusion.3
  (96 shorter events, 47.2 us)
Async XLA Ops:
  20.5 20.7 %copy-start.4 = (bf16[400,384]{1,0:T(8,128)(2,1)S(1)}, bf16[400,384]{1,0:T(8,128)(2,1)}, u32[]{:S(2)}) copy-start(bf16[400,384]{1,0:T(8,128)(2,1)} %param.10) | copy-start | bytes 921604
  41.4 34.6 %copy-start.3 = (bf16[1,136,3200]{2,1,0:T(8,128)(2,1)S(1)}, bf16[1,136,3200]{2,1,0:T(8,128)(2,1)}, u32[]{:S(2)}) copy-start(bf16[1,136,3200]{2,1,0:T(8,128)(2,1)} %param.8) | copy-start | bytes 2611204
  79.4 8.1 %copy-start.8 = (f32[2,128]{1,0:T(2,128)S(1)}, f32[2,128]{1,0:T(2,128)}, u32[]{:S(2)}) copy-start(f32[2,128]{1,0:T(2,128)} %param.11) | copy-start | bytes 3076
  79.4 104.8 %all-to-all-start = ((bf16[8,136,3200]{2,1,0:T(8,128)(2,1)}), bf16[8,136,3200]{2,1,0:T(8,128)(2,1)}, u32[]{:S(2)}, u32[]{:S(2)}) async-start(bf16[8,136,3200]{2,1,0:T(8,128)(2,1)} %stack.34), calls=%async_computation | async-start | bytes 13926400 | tf_op jit(solution)/shard_map/all_to_all | solution.py:96
  86.1 8.8 %collective-permute-start = (bf16[3200,384]{1,0:T(8,128)(2,1)S(1)}, bf16[3200,384]{1,0:T(8,128)(2,1)}, u32[]{:S(2)}, u32[]{:S(2)}) collective-permute-start(bf16[3200,384]{1,0:T(8,128)(2,1)S(1)} %bitcast.107), channel_id=1, source_target_pairs={{0,1},{1,0},{2,3},{3,2},{4,5},{5,4},{6,7},{7,6},{8,9},{9,8},{10,11... | collective-permute-start | bytes 7372808 | tf_op jit(solution)/shard_map/ppermute | solution.py:61
  87.1 5.0 %collective-permute-start.1 = (bf16[2048,200]{0,1:T(8,128)(2,1)}, bf16[2048,200]{0,1:T(8,128)(2,1)}, u32[]{:S(2)}, u32[]{:S(2)}) collective-permute-start(bf16[2048,200]{0,1:T(8,128)(2,1)} %copy_bitcast_fusion), channel_id=1, source_target_pairs={{0,1},{1,0},{2,3},{3,2},{4,5},{5,4},{6,7},{7,6},{8,9},{9,8},{10,11... | collective-permute-start | bytes 2457608 | tf_op jit(solution)/shard_map/ppermute | solution.py:61
  87.6 4.5 collective-permute-start.2
  107.0 81.6 %copy-start.5 = (f32[3200]{0:T(1024)S(1)}, f32[3200]{0:T(1024)}, u32[]{:S(2)}) copy-start(f32[3200]{0:T(1024)} %param.9) | copy-start | bytes 38404
  203.7 15.3 %all-to-all-start.4 = ((f32[8,2,1088]{2,1,0:T(2,128)}), f32[8,2,1088]{2,1,0:T(2,128)S(1)}, u32[]{:S(2)}, u32[]{:S(2)}) async-start(f32[8,2,1088]{2,1,0:T(2,128)} %broadcast_in_dim.96), calls=%async_computation.4 | async-start | bytes 147456 | tf_op jit(solution)/shard_map/all_to_all | solution.py:50
  219.0 1.1 copy-start.2
  220.3 3.0 collective-permute-start.3
  235.3 7.0 %copy-start.6 = (s32[8,2]{0,1:T(2,128)S(1)}, s32[8,2]{0,1:T(2,128)}, u32[]{:S(2)}) copy-start(s32[8,2]{0,1:T(2,128)} %param.14) | copy-start | bytes 196
  235.3 7.0 %copy-start.7 = (s32[8,2]{0,1:T(2,128)S(1)}, s32[8,2]{0,1:T(2,128)}, u32[]{:S(2)}) copy-start(s32[8,2]{0,1:T(2,128)} %param.15) | copy-start | bytes 196
  235.3 66.1 %all-to-all-start.5 = ((bf16[16,1088,128]{2,1,0:T(8,128)(2,1)}), bf16[16,1088,128]{2,1,0:T(8,128)(2,1)}, u32[]{:S(2)}, u32[]{:S(2)}) async-start(bf16[16,1088,128]{2,1,0:T(8,128)(2,1)} %bitcast.106), calls=%async_computation.5 | async-start | bytes 8912896 | tf_op jit(solution)/shard_map/all_to_all | solution.py:156
  241.3 60.0 %copy-start = (bf16[2048,400]{0,1:T(8,128)(2,1)S(1)}, bf16[2048,400]{0,1:T(8,128)(2,1)}, u32[]{:S(2)}) copy-start(bf16[2048,400]{0,1:T(8,128)(2,1)} %pad_maximum_fusion.3) | copy-start | bytes 4915204
  312.8 7.8 %copy-start.1 = (bf16[1088,400]{0,1:T(8,128)(2,1)S(1)}, bf16[1088,400]{0,1:T(8,128)(2,1)}, u32[]{:S(2)}) copy-start(bf16[1088,400]{0,1:T(8,128)(2,1)} %copy.98) | copy-start | bytes 2611204
  321.0 2.1 collective-permute-start.4
  348.4 96.5 %all-to-all-start.6 = ((bf16[8,2,256,800]{2,3,1,0:T(8,128)(2,1)}), bf16[8,2,256,800]{2,3,1,0:T(8,128)(2,1)}, u32[]{:S(2)}, u32[]{:S(2)}) async-start(bf16[8,2,256,800]{2,3,1,0:T(8,128)(2,1)} %broadcast_select_fusion), calls=%async_computation.6 | async-start | bytes 13107200 | tf_op jit(solution)/shard_map/all_to_all | solution.py:186
